TPU v7x, 32 devices: a whole 2x2x4 slice. The times are simulated.
32 devices in a mesh: ctx: 8 (over z, x), head: 4 (over y, core).
Axes of the slice: x: 2, y: 2, z: 4, core: 2. Of those that a mesh axis runs over, the one named last changes fastest.
Arguments:
- queries: bfloat16 [4096, 4096], P('ctx', 'head'), may hold values from -6 to 6
- key_states: bfloat16 [4096, 4096], P('ctx', 'head'), may hold values from -6 to 6
- value_states: bfloat16 [4096, 4096], P('ctx', 'head'), may hold values from -6 to 6
- transition_vectors: bfloat16 [4096, 4096], P('ctx', 'head'), may hold values from -6 to 6
- beta_logit: float32 [4096, 32], P('ctx', 'head'), may hold values from -6 to 6
- document_ids: int32 [4096], P('ctx'), may hold values from 0 to 7, as said below
- out_weight: bfloat16 [4096, 4096], P('head'), may hold values from -0.09375 to 0.09375
Outputs:
- layer_out: bfloat16 [4096, 4096], P(('ctx', 'head'))
Inputs may be any that keep to these rules, and one draw needn't show every extreme that they name: `document_ids`: document ids never fall along the sequence; document 0 is the first 2304 tokens; the other documents have 1 or more tokens each and together fill the rest.
All inputs are finite; a program needn't handle non-finite values.
Results may differ from a plain program's by a relative error of at most 0.022.
Values may be sent and summed in bfloat16 or wider, within the bound.
No kernel may reach another device: no remote copies, remote signals or barrier semaphores. Data moves between devices by JAX's collectives and lax.ppermute only.
A program may use at most 128 MiB of HBM per device.

v0:
```python
import jax
import jax.numpy as jnp
from jax import lax
from jax.sharding import PartitionSpec as P

epsilon = 1e-06
masked_value = -1e30
highest = lax.Precision.HIGHEST


def shard_operators(query_block, key_block, vector_block, strength):
    block_rows = key_block.shape[0]
    head_width = key_block.shape[1]
    row_ids = jnp.arange(block_rows)
    strict = row_ids[:, None] > row_ids[None, :]
    causal = row_ids[:, None] >= row_ids[None, :]
    intersections = jnp.dot(vector_block, vector_block.T, precision=highest)
    unit_lower = jnp.where(strict, intersections * strength[None, :], 0.0) + jnp.eye(
        block_rows, dtype=jnp.float32
    )
    key_proj = jnp.where(strict, jnp.dot(vector_block, key_block.T, precision=highest), 0.0)
    solved = lax.linalg.triangular_solve(
        unit_lower,
        jnp.concatenate([key_proj, vector_block], axis=1),
        left_side=True,
        lower=True,
        unit_diagonal=True,
    )
    key_solve = solved[:, :block_rows]
    vector_solve = solved[:, block_rows:]
    weighted = strength[:, None] * vector_block
    keys_end = (key_block - jnp.dot(key_solve.T, weighted, precision=highest)).astype(jnp.bfloat16)
    transfer = jnp.eye(head_width, dtype=jnp.float32) - jnp.dot(
        vector_block.T, strength[:, None] * vector_solve, precision=highest
    )
    query_dots = jnp.where(causal, jnp.dot(query_block, vector_block.T, precision=highest), 0.0)
    scaled_dots = query_dots * strength[None, :]
    intra_scores = jnp.dot(query_block, key_block.T, precision=highest) - jnp.dot(
        scaled_dots, key_solve, precision=highest
    )
    rotated = query_block - jnp.dot(scaled_dots, vector_solve, precision=highest)
    return (intra_scores, keys_end, transfer, rotated)


def on_device(
    queries, key_states, value_states, transition_vectors, beta_logit, document_ids, out_weight
):
    block_rows = queries.shape[0]
    head_count = beta_logit.shape[1]
    head_width = queries.shape[1] // head_count
    score_scale = head_width ** (-0.5)

    def split_heads(flat):
        return jnp.transpose(flat.reshape(block_rows, head_count, head_width), (1, 0, 2))

    query_heads = split_heads(queries).astype(jnp.float32)
    key_heads = split_heads(key_states).astype(jnp.float32)
    value_heads = split_heads(value_states)
    vector_heads = split_heads(transition_vectors).astype(jnp.float32)
    unit_vectors = vector_heads / jnp.sqrt(
        jnp.sum(vector_heads * vector_heads, axis=2, keepdims=True) + epsilon
    )
    strength = 2.0 * jax.nn.sigmoid(beta_logit.T)
    intra_scores, keys_end, transfer, rotated = jax.vmap(shard_operators)(
        query_heads, key_heads, unit_vectors, strength
    )
    row_ids = jnp.arange(block_rows)
    causal = row_ids[:, None] >= row_ids[None, :]
    doc_float = (document_ids + 1).astype(jnp.float32)
    same_doc = doc_float[:, None] == doc_float[None, :]
    own_scores = jnp.where((causal & same_doc)[None], intra_scores * score_scale, masked_value)
    running_max = jnp.max(own_scores, axis=2)
    weights = jnp.exp(own_scores - running_max[..., None])
    running_sum = jnp.sum(weights, axis=2)
    accumulated = jnp.einsum(
        "hqk,hkd->hqd",
        weights.astype(jnp.bfloat16),
        value_heads,
        preferred_element_type=jnp.float32,
    )
    ctx_index = lax.axis_index("ctx")
    ctx_count = lax.axis_size("ctx")
    packed = jnp.stack([keys_end, value_heads])

    def attend(carried, key_pair, transfer_in, key_docs, is_live):
        turned, running_max, running_sum, accumulated = carried
        scores = jnp.einsum(
            "hqd,hkd->hqk",
            turned.astype(jnp.bfloat16),
            key_pair[0],
            preferred_element_type=jnp.float32,
        )
        allowed = (doc_float[:, None] == key_docs[None, :]) & is_live
        scores = jnp.where(allowed[None], scores * score_scale, masked_value)
        new_max = jnp.maximum(running_max, jnp.max(scores, axis=2))
        factor = jnp.exp(running_max - new_max)
        weights = jnp.exp(scores - new_max[..., None])
        running_sum = running_sum * factor + jnp.sum(weights, axis=2)
        accumulated = accumulated * factor[..., None] + jnp.einsum(
            "hqk,hkd->hqd",
            weights.astype(jnp.bfloat16),
            key_pair[1],
            preferred_element_type=jnp.float32,
        )
        turned = jnp.einsum("hqd,hde->hqe", turned, transfer_in, precision=highest)
        return (turned, new_max, running_sum, accumulated)

    def visit(carried, key_pair, transfer_in, key_docs, is_live):
        return attend(carried, key_pair, transfer_in, key_docs, is_live)

    carried = (rotated, running_max, running_sum, accumulated)
    every_pair = lax.all_gather(packed, "ctx", axis=2, tiled=True)
    every_transfer, every_doc = (
        lax.all_gather(transfer[None].astype(jnp.bfloat16), "ctx", axis=0, tiled=True).astype(
            jnp.float32
        ),
        lax.all_gather(doc_float.astype(jnp.bfloat16), "ctx", axis=0, tiled=True).astype(
            doc_float.dtype
        ),
    )

    def local_step(offset, inner):
        source = jnp.maximum(ctx_index - offset, 0)
        key_pair = lax.dynamic_slice_in_dim(every_pair, source * block_rows, block_rows, 2)
        transfer_in = lax.dynamic_index_in_dim(every_transfer, source, 0, keepdims=False)
        key_docs = lax.dynamic_slice_in_dim(every_doc, source * block_rows, block_rows, 0)
        return visit(inner, key_pair, transfer_in, key_docs, ctx_index - offset >= 0)

    carried = lax.fori_loop(1, ctx_count, local_step, carried)
    attended = (carried[3] / carried[2][..., None]).astype(jnp.bfloat16)
    token_rows = jnp.transpose(attended, (1, 0, 2)).reshape(block_rows, head_count * head_width)
    return lax.psum_scatter(
        jnp.dot(token_rows, out_weight, preferred_element_type=jnp.float32).astype(jnp.bfloat16),
        "head",
        scatter_dimension=0,
        tiled=True,
    )


def solution(mesh):
    return jax.shard_map(
        on_device,
        mesh=mesh,
        in_specs=(
            P("ctx", "head"),
            P("ctx", "head"),
            P("ctx", "head"),
            P("ctx", "head"),
            P("ctx", "head"),
            P("ctx"),
            P("head", None),
        ),
        out_specs=P(("ctx", "head"), None),
        check_vma=False,
    )
```

profile of v0, /device:TPU:16, one launch (start us, length us, event | category | flops | bytes accessed | tf_op | source)
XLA Modules:
  0.0 894.2 jit_solution(15207088580192670057)
XLA Ops:
  16.1 6.1 broadcast_select_fusion
  22.2 11.6 %select_add_fusion = f32[8,512,512]{1,2,0:T(8,128)} fusion(f32[512,512]{0,1:T(8,128)S(1)} %copy-done.22, f32[512,512]{0,1:T(8,128)S(1)} %copy-done.21, f32[8,512]{1,0:T(8,128)S(1)} %multiply_bitcast_fusion, pred[512,512]{0,1:T(8,128)(4,1)S(1)} %get-tuple-element.265, pred[512,512]{0,1:T(8,128)(4,1)S(1)} %copy-done.23, ...), kind=kOutput, calls=%fused_computation.42 | convolution fusion | flops 3231711232 | bytes 13123584 | tf_op jit(solution)/shard_map/vmap()/dot_general | solution.py:17
  33.8 17.5 %while.21 = (s32[]{:T(128)}, f32[8,512,512]{1,2,0:T(8,128)}, s32[4,2]{0,1:T(2,128)S(1)}, f32[4,8,128,128]{3,2,0,1:T(8,128)}, s32[]{:T(128)}) while((s32[]{:T(128)}, f32[8,512,512]{1,2,0:T(8,128)}, s32[4,2]{0,1:T(2,128)S(1)}, f32[4,8,128,128]{3,2,0,1:T(8,128)}, s32[]{:T(128)}) %tuple.58), condition=%wide.while_cond, body=%wide.while_body.sunk | while | flops 2 | bytes 3145845 | solution.py:22
  51.3 316.0 %custom-call.3 = f32[8,4,128,128]{2,3,1,0:T(8,128)} custom-call(f32[8,4,128,128]{3,2,1,0:T(8,128)} %bitcast.132), custom_call_target="InvertDiagBlocksLowerTriangular" | custom-call | tf_op jit(solution)/shard_map/vmap()/triangular_solve | solution.py:22
  372.1 6.0 fusion.90
  378.1 4.8 fusion.56
  382.9 11.1 %fusion.33 = f32[8,128,640]{1,2,0:T(8,128)S(1)} fusion(f32[8,128,640]{2,1,0:T(8,128)S(1)} %fusion.56, f32[8,128,640]{2,1,0:T(8,128)S(1)} %fusion.52, f32[8,512,512]{1,2,0:T(8,128)} %get-tuple-element.434), kind=kOutput, calls=%fused_computation.54 | convolution fusion | flops 2014576640 | bytes 8912896 | tf_op jit(solution)/shard_map/vmap()/triangular_solve | solution.py:22
  398.6 16.0 %fusion.21 = f32[8,128,640]{1,2,0:T(8,128)} fusion(f32[8,128,640]{2,1,0:T(8,128)S(1)} %fusion.49, f32[8,128,640]{2,1,0:T(8,128)S(1)} %fusion.56, f32[8,128,640]{2,1,0:T(8,128)S(1)} %fusion.52, f32[8,512,512]{1,2,0:T(8,128)} %get-tuple-element.434), kind=kOutput, calls=%fused_computation.43 | convolution fusion | flops 3023831040 | bytes 12058624 | tf_op jit(solution)/shard_map/vmap()/triangular_solve | solution.py:22
  424.4 5.2 fusion.59
  438.4 10.1 %fusion.70 = bf16[1,8,512,128]{3,2,1,0:T(8,128)(2,1)S(1)} fusion(f32[8,512,128]{1,2,0:T(8,128)S(1)} %broadcast_divide_fusion, f32[8,128,640]{1,2,0:T(8,128)} %copy-done.8, f32[8,128,640]{1,2,0:T(8,128)} %copy.108, f32[8,128,640]{1,2,0:T(8,128)} %copy.107, f32[8,128,640]{1,2,0:T(8,128)} %copy.106, bf16[512,8,128]{2,0,1:T(8,128)(2,1)} %copy-done.14, ...), kind=kOutput, calls=%fused_computation.90 | convolution fusion | flops 3229614080 | bytes 14696448 | tf_op jit(solution)/shard_map/vmap()/dot_general | solution.py:32
  461.6 15.8 %convert_subtract_fusion = f32[8,512,128]{2,1,0:T(8,128)} fusion(f32[8,512,128]{1,2,0:T(8,128)S(1)} %copy-done.7, f32[8,512,512]{2,1,0:T(8,128)S(1)} %fusion.84, f32[8,512]{1,0:T(8,128)S(1)} %multiply_bitcast_fusion, pred[512,512]{0,1:T(8,128)(4,1)S(1)} %iota_compare_fusion.4, bf16[512,8,128]{2,0,1:T(8,128)(2,1)S(1)} %copy.81), kind=kOutput, calls=%fused_computation.88 | convolution fusion | flops 3226468352 | bytes 13910016 | tf_op jit(solution)/shard_map/vmap()/dot_general | solution.py:41
  479.4 23.7 %all-gather.1 = bf16[8,1,512]{2,1,0:T(2,128)(2,1)S(1)} all-gather(bf16[1,1,512]{2,1,0:T(2,128)(2,1)S(1)} %reshape.148), channel_id=1, replica_groups=mesh['ctx'=8,'head'=4] {'ctx'}, dimensions={0}, use_global_device_ids=true | all-gather | bytes 9216 | tf_op jit(solution)/shard_map/all_gather | solution.py:117
  503.3 17.9 %fusion.29 = f32[8,512,512]{1,2,0:T(8,128)S(1)} fusion(f32[8,512,512]{2,1,0:T(8,128)} %copy-done.3, f32[8,512]{1,0:T(8,128)S(1)} %multiply_bitcast_fusion, pred[512,512]{0,1:T(8,128)(4,1)S(1)} %iota_compare_fusion.4, f32[8,128,640]{1,2,0:T(8,128)} %copy-done.8, f32[8,128,640]{1,2,0:T(8,128)} %copy.108, f32[8,128,640]{1,2,0:T(8,128)} %copy.107, ...), kind=kOutput, calls=%fused_computation.51 | convolution fusion | flops 12895387648 | bytes 27541504 | tf_op jit(solution)/shard_map/vmap()/dot_general | solution.py:38
  531.5 181.9 %all-gather.5.cloned.1.call-done = bf16[2,8,4096,128]{3,2,1,0:T(8,128)(2,1)} async-done(((bf16[2,8,512,128]{3,2,1,0:T(8,128)(2,1)}), bf16[2,8,4096,128]{3,2,1,0:T(8,128)(2,1)}) %all-gather.5.cloned.1.call-update) | async-done | bytes 16777232 | tf_op jit(solution)/shard_map/all_gather | solution.py:112
  713.4 118.4 %while.20 = (s32[]{:T(128)}, f32[8,512,128]{1,2,0:T(8,128)S(1)}, f32[8,512]{1,0:T(8,128)S(1)}, f32[8,512]{1,0:T(8,128)S(1)}, f32[8,512,128]{2,1,0:T(8,128)}, /*i...) while((s32[]{:T(128)}, f32[8,512,128]{1,2,0:T(8,128)S(1)}, ...), condition=%wide.region_6.7_spmd, body=%wide.region_3.6_spmd.sunk | while | flops 1904222208 | bytes 77340952 | solution.py:129
  722.1 8.4 multiply_add_fusion.5
  739.0 8.4 multiply_add_fusion.5
  755.9 8.4 multiply_add_fusion.5
  772.7 8.4 multiply_add_fusion.5
  789.6 8.4 multiply_add_fusion.5
  806.5 8.4 multiply_add_fusion.5
  823.4 8.4 multiply_add_fusion.5
  834.0 9.5 %convolution_convert_fusion = bf16[512,4096]{1,0:T(8,128)(2,1)} fusion(bf16[512,1024]{0,1:T(8,128)(2,1)S(1)} %bitcast.130, bf16[1024,4096]{1,0:T(8,128)(2,1)} %param.15), kind=kOutput, calls=%fused_computation.53 | convolution fusion | flops 4297064448 | bytes 13631488 | tf_op jit(solution)/shard_map/dot_general | solution.py:133
  843.5 43.8 %reduce-scatter.2.cloned.1.call-done = bf16[128,4096]{1,0:T(8,128)(2,1)} async-done(((bf16[512,4096]{1,0:T(8,128)(2,1)}), bf16[128,4096]{1,0:T(8,128)(2,1)}) %reduce-scatter.2.cloned.1.call-update) | async-done | bytes 1048592 | tf_op jit(solution)/shard_map/reduce_scatter | solution.py:132
  (198 shorter events, 141.3 us)
Async XLA Ops:
  6.5 520.8 %all-gather.7.cloned.1.call-start = ((), (), s32[]{:S(2)}) async-start(), calls=%async_computation.3 | async-start | bytes 2359296 | tf_op jit(solution)/shard_map/all_gather | solution.py:114
  16.0 6.2 copy-start.14
  16.0 6.2 copy-start.21
  16.0 6.1 copy-start.22
  16.1 6.1 copy-start.23
  367.3 10.7 %copy-start.16 = (f32[8,4,128,128]{2,3,1,0:T(8,128)S(1)}, f32[8,4,128,128]{2,3,1,0:T(8,128)}, u32[]{:S(2)}) copy-start(f32[8,4,128,128]{2,3,1,0:T(8,128)} %custom-call.3) | copy-start | bytes 6291460
  372.1 24.9 %copy-start.1 = (f32[8,128,640]{2,1,0:T(8,128)}, f32[8,128,640]{2,1,0:T(8,128)S(1)}, u32[]{:S(2)}) copy-start(f32[8,128,640]{2,1,0:T(8,128)S(1)} %fusion.52) | copy-start | bytes 7864324
  372.1 21.9 %slice-start = ((s8[8388608]{0:T(1024)(128)(4,1)}), s8[4194304]{0:T(1024)(128)(4,1)S(1)}, s32[]{:S(2)}) async-start(s8[8388608]{0:T(1024)(128)(4,1)} %bitcast.123), calls=%async_computation.4 | async-start | bytes 8388608
  378.1 15.9 %slice-start.1 = ((s8[8388608]{0:T(1024)(128)(4,1)}), s8[4194304]{0:T(1024)(128)(4,1)S(1)}, s32[]{:S(2)}) async-start(s8[8388608]{0:T(1024)(128)(4,1)} %bitcast.123), calls=%async_computation.5 | async-start | bytes 8388608
  382.8 14.1 %copy-start.2 = (f32[8,128,640]{2,1,0:T(8,128)}, f32[8,128,640]{2,1,0:T(8,128)S(1)}, u32[]{:S(2)}) copy-start(f32[8,128,640]{2,1,0:T(8,128)S(1)} %fusion.56) | copy-start | bytes 7864324
  424.4 5.2 copy-start.9
  424.4 5.2 copy-start.10
  424.4 5.2 copy-start.11
  435.4 278.0 %all-gather.5.cloned.1.call-start = ((), (), s32[]{:S(2)}) async-start(), calls=%async_computation.1 | async-start | bytes 18874368 | tf_op jit(solution)/shard_map/all_gather | solution.py:112
  438.4 10.1 %copy-start.12 = (bf16[512,8,128]{2,0,1:T(8,128)(2,1)}, bf16[512,8,128]{2,0,1:T(8,128)(2,1)S(1)}, u32[]{:S(2)}) copy-start(bf16[512,8,128]{2,0,1:T(8,128)(2,1)S(1)} %copy.114) | copy-start | bytes 3145732
  450.0 437.3 %reduce-scatter.2.cloned.1.call-start = ((), (), s32[]{:S(2)}) async-start(), calls=%async_computation.2 | async-start | bytes 5242880 | tf_op jit(solution)/shard_map/reduce_scatter | solution.py:132
  454.7 6.9 copy-start.7
  503.3 17.9 %copy-start.15 = (bf16[512,8,128]{2,0,1:T(8,128)(2,1)S(1)}, bf16[512,8,128]{2,0,1:T(8,128)(2,1)}, u32[]{:S(2)}) copy-start(bf16[512,8,128]{2,0,1:T(8,128)(2,1)} %copy-done.14) | copy-start | bytes 3145732
  716.9 5.2 copy-start
  733.7 5.2 copy-start
  750.6 5.2 copy-start
  767.5 5.2 copy-start
  784.4 5.2 copy-start
  801.3 5.2 copy-start
  (13 other events, 29.2 us)
Sparse Core Ops, SparseCore 0:
  435.5 49.7 all-gather.6
  487.5 225.8 all-gather.4
  843.6 43.5 reduce-scatter.1
where the time goes:
time: 905 us; the launch traced here: 894 us
  other arithmetic  343 us (38%)
  matrix products  235 us (26%)
  waiting for transfers between devices  226 us (25%)
  local copies, waits for them, and re-layouts  52.6 us (6%)
  blocking collectives  23.7 us (3%)
  between operations  14 us (2%)
    another operation x3, other arithmetic, shard_operators(): lax.linalg.triangular_solve(unit_lower, jnp.concatenate([key_proj, vector...  316 us
    all_gather x1, waiting for transfers between devices, on_device(): every_pair = lax.all_gather(packed, 'ctx', axis=2, tiled=True)  182 us
    dot_general x7, matrix products, attend(): jnp.einsum('hqk,hkd->hqd', weights.astype(jnp.bfloat16), key_pair[1], pre...  58.8 us
    another operation x7, matrix products, shard_operators(): lax.linalg.triangular_solve(unit_lower, jnp.concatenate([key_proj, vector...  50.7 us
    reduce_scatter x1, waiting for transfers between devices, on_device(): lax.psum_scatter(jnp.dot(token_rows, out_weight, preferred_element_type=j...  43.8 us
    dot_general x7, matrix products, attend(): turned = jnp.einsum('hqd,hde->hqe', turned, transfer_in, precision=highest)  23.7 us
    all_gather x1, blocking collectives, on_device(): lax.all_gather(doc_float.astype(jnp.bfloat16), 'ctx', axis=0, tiled=True)  23.7 us
    dot_general x7, matrix products, attend(): jnp.einsum('hqd,hkd->hqk', turned.astype(jnp.bfloat16), key_pair[0], pref...  19.3 us
  transfers between devices with their start and end apart: 3, of which 2 were waited for; matrix products, arithmetic and copies ran while one was open for 8% of the time, Pallas kernels for 0%

commit v1 on v0

--- a/solution.py
+++ b/solution.py
@@ -8,6 +8,56 @@
 highest = lax.Precision.HIGHEST
 
 
+def diagonal_blocks(matrix, size):
+    count = matrix.shape[0] // size
+    tiled = matrix.reshape(count, size, count, size)
+    mask = jnp.eye(count, dtype=bool)[:, None, :, None]
+    return jnp.sum(jnp.where(mask, tiled, 0.0), axis=2)
+
+
+def unit_lower_inverse(strict_lower):
+    rows_total = strict_lower.shape[0]
+    leaf = 16
+    leaves = diagonal_blocks(strict_lower, leaf)
+    rows = []
+    for i in range(leaf):
+        row = jnp.broadcast_to((jnp.arange(leaf) == i).astype(jnp.float32), leaves.shape[:1] + (leaf,))
+        for m in range(i):
+            row = row - leaves[:, i, m][:, None] * rows[m]
+        rows.append(row)
+    inverse = jnp.stack(rows, axis=1)
+    size = leaf
+    while size < rows_total:
+        pairs = rows_total // (2 * size)
+        lower = diagonal_blocks(strict_lower, 2 * size)[:, size:, :size]
+        halves = inverse.reshape(pairs, 2, size, size)
+        first = halves[:, 0]
+        second = halves[:, 1]
+        corner = -jnp.einsum(
+            "pij,pjk->pik",
+            second,
+            jnp.einsum("pij,pjk->pik", lower, first, precision=highest),
+            precision=highest,
+        )
+        top = jnp.concatenate([first, jnp.zeros_like(first)], axis=2)
+        bottom = jnp.concatenate([corner, second], axis=2)
+        inverse = jnp.concatenate([top, bottom], axis=1)
+        size *= 2
+    return inverse[0]
+
+
+def lower_solve(strict_lower, right):
+    rows_total = strict_lower.shape[0]
+    leaf = 16
+    count = rows_total // leaf
+    if rows_total % leaf or count & (count - 1):
+        unit_lower = strict_lower + jnp.eye(rows_total, dtype=jnp.float32)
+        return lax.linalg.triangular_solve(
+            unit_lower, right, left_side=True, lower=True, unit_diagonal=True
+        )
+    return jnp.dot(unit_lower_inverse(strict_lower), right, precision=highest)
+
+
 def shard_operators(query_block, key_block, vector_block, strength):
     block_rows = key_block.shape[0]
     head_width = key_block.shape[1]
@@ -15,17 +65,9 @@
     strict = row_ids[:, None] > row_ids[None, :]
     causal = row_ids[:, None] >= row_ids[None, :]
     intersections = jnp.dot(vector_block, vector_block.T, precision=highest)
-    unit_lower = jnp.where(strict, intersections * strength[None, :], 0.0) + jnp.eye(
-        block_rows, dtype=jnp.float32
-    )
+    strict_lower = jnp.where(strict, intersections * strength[None, :], 0.0)
     key_proj = jnp.where(strict, jnp.dot(vector_block, key_block.T, precision=highest), 0.0)
-    solved = lax.linalg.triangular_solve(
-        unit_lower,
-        jnp.concatenate([key_proj, vector_block], axis=1),
-        left_side=True,
-        lower=True,
-        unit_diagonal=True,
-    )
+    solved = lower_solve(strict_lower, jnp.concatenate([key_proj, vector_block], axis=1))
     key_solve = solved[:, :block_rows]
     vector_solve = solved[:, block_rows:]
     weighted = strength[:, None] * vector_block
@@ -80,14 +122,14 @@
     )
     ctx_index = lax.axis_index("ctx")
     ctx_count = lax.axis_size("ctx")
-    packed = jnp.stack([keys_end, value_heads])
+    every_value = lax.all_gather(value_heads, "ctx", axis=1, tiled=True)
 
-    def attend(carried, key_pair, transfer_in, key_docs, is_live):
+    def attend(carried, key_pair, value_pair, transfer_in, key_docs, is_live):
         turned, running_max, running_sum, accumulated = carried
         scores = jnp.einsum(
             "hqd,hkd->hqk",
             turned.astype(jnp.bfloat16),
-            key_pair[0],
+            key_pair,
             preferred_element_type=jnp.float32,
         )
         allowed = (doc_float[:, None] == key_docs[None, :]) & is_live
@@ -99,17 +141,17 @@
         accumulated = accumulated * factor[..., None] + jnp.einsum(
             "hqk,hkd->hqd",
             weights.astype(jnp.bfloat16),
-            key_pair[1],
+            value_pair,
             preferred_element_type=jnp.float32,
         )
         turned = jnp.einsum("hqd,hde->hqe", turned, transfer_in, precision=highest)
         return (turned, new_max, running_sum, accumulated)
 
-    def visit(carried, key_pair, transfer_in, key_docs, is_live):
-        return attend(carried, key_pair, transfer_in, key_docs, is_live)
+    def visit(carried, key_pair, value_pair, transfer_in, key_docs, is_live):
+        return attend(carried, key_pair, value_pair, transfer_in, key_docs, is_live)
 
     carried = (rotated, running_max, running_sum, accumulated)
-    every_pair = lax.all_gather(packed, "ctx", axis=2, tiled=True)
+    every_key = lax.all_gather(keys_end, "ctx", axis=1, tiled=True)
     every_transfer, every_doc = (
         lax.all_gather(transfer[None].astype(jnp.bfloat16), "ctx", axis=0, tiled=True).astype(
             jnp.float32
@@ -121,10 +163,11 @@
 
     def local_step(offset, inner):
         source = jnp.maximum(ctx_index - offset, 0)
-        key_pair = lax.dynamic_slice_in_dim(every_pair, source * block_rows, block_rows, 2)
+        key_pair = lax.dynamic_slice_in_dim(every_key, source * block_rows, block_rows, 1)
+        value_pair = lax.dynamic_slice_in_dim(every_value, source * block_rows, block_rows, 1)
         transfer_in = lax.dynamic_index_in_dim(every_transfer, source, 0, keepdims=False)
         key_docs = lax.dynamic_slice_in_dim(every_doc, source * block_rows, block_rows, 0)
-        return visit(inner, key_pair, transfer_in, key_docs, ctx_index - offset >= 0)
+        return visit(inner, key_pair, value_pair, transfer_in, key_docs, ctx_index - offset >= 0)
 
     carried = lax.fori_loop(1, ctx_count, local_step, carried)
     attended = (carried[3] / carried[2][..., None]).astype(jnp.bfloat16)

time: 905 us -> 1100 us (1.22); the launches traced: 894 us -> 1080 us
  local copies, waits for them, and re-layouts: 52.6 us -> 449 us
  other arithmetic: 343 us -> 130 us
  matrix products: 235 us -> 215 us
  waiting for transfers between devices: 226 us -> 241 us
    another operation x4 -> x1, other arithmetic: 318 us -> 4.84 us  [unit_lower_inverse(): inverse = jnp.stack(rows, axis=1)]
    slice x0 -> x132, local copies, waits for them, and re-layouts: none -> 217 us  [the longest x127 211 us: unit_lower_inverse(): row = row - leaves[:, i, m][:, None] * rows[m]]
    mul x0 -> x120, local copies, waits for them, and re-layouts: none -> 97 us  [unit_lower_inverse(): row = row - leaves[:, i, m][:, None] * rows[m]]
    reshape x0 -> x5, local copies, waits for them, and re-layouts: none -> 92.6 us  [diagonal_blocks(): tiled = matrix.reshape(count, size, count, size)]
    reduce_sum x0 -> x5, other arithmetic: none -> 64.2 us  [diagonal_blocks(): return jnp.sum(jnp.where(mask, tiled, 0.0), axis=2)]
    another operation x7 -> x0, matrix products: 50.7 us -> none  [shard_operators(): lax.linalg.triangular_solve(unit_lower, jnp.concatenate([key_proj, vector...]
    unnamed x2 -> x14, other arithmetic: 0.01 us -> 30.7 us
    another operation x24 -> x14, local copies, waits for them, and re-layouts: 27.3 us -> 1.23 us
  transfers between devices with their start and end apart: 3 -> 4, of which waited for: 2 -> 3; matrix products, arithmetic and copies ran while one was open for 8% -> 7% of each run, Pallas kernels for 0% -> 0%
where the time goes in v1:
time: 1100 us; the launch traced here: 1080 us
  local copies, waits for them, and re-layouts  449 us (41%)
  waiting for transfers between devices  241 us (22%)
  matrix products  215 us (20%)
  other arithmetic  130 us (12%)
  blocking collectives  23.7 us (2%)
  between operations  15.2 us (1%)
    slice x127, local copies, waits for them, and re-layouts, unit_lower_inverse(): row = row - leaves[:, i, m][:, None] * rows[m]  211 us
    all_gather x1, waiting for transfers between devices, on_device(): every_value = lax.all_gather(value_heads, 'ctx', axis=1, tiled=True)  126 us
    mul x120, local copies, waits for them, and re-layouts, unit_lower_inverse(): row = row - leaves[:, i, m][:, None] * rows[m]  97 us
    reshape x5, local copies, waits for them, and re-layouts, diagonal_blocks(): tiled = matrix.reshape(count, size, count, size)  92.6 us
    all_gather x1, waiting for transfers between devices, on_device(): every_key = lax.all_gather(keys_end, 'ctx', axis=1, tiled=True)  71.1 us
    reduce_sum x5, other arithmetic, diagonal_blocks(): return jnp.sum(jnp.where(mask, tiled, 0.0), axis=2)  64.2 us
    reduce_scatter x1, waiting for transfers between devices, on_device(): lax.psum_scatter(jnp.dot(token_rows, out_weight, preferred_element_type=j...  43.8 us
    unnamed x14, other arithmetic  30.7 us
  transfers between devices with their start and end apart: 4, of which 3 were waited for; matrix products, arithmetic and copies ran while one was open for 7% of the time, Pallas kernels for 0%

profile of v1, /device:TPU:16, one launch (start us, length us, event | category | flops | bytes accessed | tf_op | source)
XLA Modules:
  0.0 1075.2 jit_solution(17737255387501927683)
XLA Ops:
  12.2 9.7 multiply_select_fusion.1
  21.9 9.1 copy.491
  31.0 38.0 %reshape.2370 = f32[8,32,16,32,16]{4,3,2,1,0:T(8,128)} reshape(f32[8,512,512]{2,1,0:T(8,128)} %copy.491) | data formatting | bytes 16777216 | tf_op jit(solution)/shard_map/vmap()/reshape | solution.py:13
  69.0 21.5 %select_reduce_fusion = f32[8,32,16,16]{3,2,1,0:T(8,128)S(1)} fusion(f32[8,32,16,32,16]{4,3,2,1,0:T(8,128)} %reshape.2370, pred[32,32]{1,0:T(8,128)(4,1)S(1)} %iota_compare_fusion.9), kind=kLoop, calls=%fused_computation.26 | loop fusion | flops 4128768 | bytes 8651776 | tf_op jit(solution)/shard_map/vmap()/reduce_sum | solution.py:15
  105.5 6.1 fusion.117
  118.6 6.2 fusion.115
  131.3 20.9 %reshape.2371 = f32[8,16,32,16,32]{2,1,4,3,0:T(8,128)} reshape(f32[8,512,512]{1,2,0:T(8,128)} %multiply_select_fusion.1) | data formatting | bytes 16777216 | tf_op jit(solution)/shard_map/vmap()/reshape | solution.py:13
  152.8 12.9 %reshape.2373 = f32[8,8,64,8,64]{2,1,4,3,0:T(8,128)} reshape(f32[8,512,512]{1,2,0:T(8,128)} %multiply_select_fusion.1) | data formatting | bytes 16777216 | tf_op jit(solution)/shard_map/vmap()/reshape | solution.py:13
  166.2 9.9 reshape.2375
  176.6 10.9 %reshape.2377 = f32[8,2,256,2,256]{2,1,4,3,0:T(2,128)} reshape(f32[8,512,512]{1,2,0:T(8,128)} %multiply_select_fusion.1) | data formatting | bytes 16777216 | tf_op jit(solution)/shard_map/vmap()/reshape | solution.py:13
  497.1 13.7 %select_reduce_fusion.1 = f32[8,16,32,32]{2,1,3,0:T(8,128)S(1)} fusion(f32[8,16,32,16,32]{2,1,4,3,0:T(8,128)} %reshape.2371, pred[16,16]{0,1:T(8,128)(4,1)S(1)} %copy-done.75), kind=kLoop, calls=%fused_computation.27 | loop fusion | flops 4063232 | bytes 8913152 | tf_op jit(solution)/shard_map/vmap()/reduce_sum | solution.py:15
  517.6 9.5 select_reduce_fusion.2
  532.7 6.7 select_reduce_fusion.4
  543.7 12.9 %select_reduce_fusion.3 = f32[8,2,256,256]{2,1,3,0:T(2,128)} fusion(f32[8,2,256,2,256]{2,1,4,3,0:T(2,128)} %reshape.2377, pred[2,2]{0,1:T(4,128)(4,1)S(1)} %copy-done.78), kind=kLoop, calls=%fused_computation.44 | loop fusion | flops 3145728 | bytes 12582916 | tf_op jit(solution)/shard_map/vmap()/reduce_sum | solution.py:15
  583.3 26.1 %fusion.22 = f32[8,512,640]{2,1,0:T(8,128)} fusion(f32[8,512,128]{1,2,0:T(8,128)S(1)} %copy-done.1, f32[8,512,512]{1,2,0:T(8,128)} %broadcast_select_fusion, f32[8,1,256,256]{3,2,0,1:T(8,128)} %get-tuple-element.265, f32[8,1,256,256]{3,2,0,1:T(8,128)} %get-tuple-element.264, f32[8,1,256,256]{3,2,0,1:T(8,128)} %negate_bitcast_fusion), kind=kOutput, calls=%fused_computation.29 | convolution fusion | flops 16117137408 | bytes 27262976 | tf_op jit(solution)/shard_map/vmap()/dot_general | solution.py:58
  620.4 16.5 %subtract_convert_fusion = bf16[8,512,128]{2,1,0:T(8,128)(2,1)} fusion(f32[8,512,128]{1,2,0:T(8,128)S(1)} %copy-done.1, f32[8,512,640]{2,1,0:T(8,128)} %fusion.22, bf16[512,8,128]{2,0,1:T(8,128)(2,1)S(1)} %copy.753, f32[8,512]{1,0:T(8,128)S(1)} %copy-done.10), kind=kOutput, calls=%fused_computation.81 | convolution fusion | flops 3223322624 | bytes 12599296 | tf_op jit(solution)/shard_map/vmap()/dot_general | solution.py:74
  652.3 16.7 %convert_subtract_fusion = f32[8,512,128]{2,1,0:T(8,128)} fusion(f32[8,512,512]{2,1,0:T(8,128)S(1)} %fusion.88, f32[8,512]{1,0:T(8,128)S(1)} %copy-done.10, pred[512,512]{0,1:T(8,128)(4,1)S(1)} %iota_compare_fusion.7, bf16[512,8,128]{2,0,1:T(8,128)(2,1)S(1)} %copy-done.3, f32[8,512,640]{2,1,0:T(8,128)} %fusion.22), kind=kOutput, calls=%fused_computation.87 | convolution fusion | flops 3226468352 | bytes 13910016 | tf_op jit(solution)/shard_map/vmap()/dot_general | solution.py:83
  671.0 23.7 %all-gather.1 = bf16[8,1,512]{2,1,0:T(2,128)(2,1)S(1)} all-gather(bf16[1,1,512]{2,1,0:T(2,128)(2,1)S(1)} %reshape.2388), channel_id=1, replica_groups=mesh['ctx'=8,'head'=4] {'ctx'}, dimensions={0}, use_global_device_ids=true | all-gather | bytes 9216 | tf_op jit(solution)/shard_map/all_gather | solution.py:159
  694.9 19.2 %fusion.35 = f32[8,512,512]{1,2,0:T(8,128)S(1)} fusion(f32[8,512,640]{2,1,0:T(8,128)} %fusion.22, f32[8,512,512]{2,1,0:T(8,128)} %copy-done.2, f32[8,512]{1,0:T(8,128)S(1)} %copy-done.10, pred[512,512]{0,1:T(8,128)(4,1)S(1)} %iota_compare_fusion.7), kind=kOutput, calls=%fused_computation.49 | convolution fusion | flops 12889096192 | bytes 25444352 | tf_op jit(solution)/shard_map/vmap()/dot_general | solution.py:80
  724.8 71.1 %all-gather.6.cloned.1.call-done = bf16[8,4096,128]{2,1,0:T(8,128)(2,1)} async-done(((bf16[8,512,128]{2,1,0:T(8,128)(2,1)}), bf16[8,4096,128]{2,1,0:T(8,128)(2,1)}) %all-gather.6.cloned.1.call-update) | async-done | bytes 8388624 | tf_op jit(solution)/shard_map/all_gather | solution.py:154
  795.8 125.7 %all-gather.8.cloned.1.call-done = bf16[8,4096,128]{1,2,0:T(8,128)(2,1)} async-done(((bf16[8,512,128]{1,2,0:T(8,128)(2,1)}), bf16[8,4096,128]{1,2,0:T(8,128)(2,1)}) %all-gather.8.cloned.1.call-update) | async-done | bytes 8388624 | tf_op jit(solution)/shard_map/all_gather | solution.py:125
  921.5 91.1 %while.19 = (s32[]{:T(128)}, f32[8,512,128]{1,2,0:T(8,128)S(1)}, f32[8,512]{1,0:T(8,128)S(1)}, f32[8,512]{1,0:T(8,128)S(1)}, f32[8,512,128]{2,1,0:T(8,128)}, /*i...) while((s32[]{:T(128)}, f32[8,512,128]{1,2,0:T(8,128)S(1)}, ...), condition=%wide.region_11.12_spmd, body=%wide.region_8.11_spmd.sunk | while | flops 1904222208 | bytes 60563748 | solution.py:172
  1014.8 9.5 convolution_convert_fusion
  1024.4 43.8 %reduce-scatter.2.cloned.1.call-done = bf16[128,4096]{1,0:T(8,128)(2,1)} async-done(((bf16[512,4096]{1,0:T(8,128)(2,1)}), bf16[128,4096]{1,0:T(8,128)(2,1)}) %reduce-scatter.2.cloned.1.call-update) | async-done | bytes 1048592 | tf_op jit(solution)/shard_map/reduce_scatter | solution.py:175
  (592 shorter events, 518.8 us)
Async XLA Ops:
  6.5 713.8 %all-gather.10.cloned.1.call-start = ((), (), s32[]{:S(2)}) async-start(), calls=%async_computation.4 | async-start | bytes 2359296 | tf_op jit(solution)/shard_map/all_gather | solution.py:156
  7.2 181.8 %copy-start.41 = (f32[16]{0:T(128)}, f32[16]{0:T(128)S(1)}, u32[]{:S(2)}) copy-start(f32[16]{0:T(128)S(1)} %get-tuple-element.399) | copy-start | bytes 196
  454.5 21.1 %copy-start.17 = (f32[8,16,2]{1,2,0:T(2,128)S(1)}, f32[8,16,2]{1,2,0:T(2,128)}, u32[]{:S(2)}) copy-start(f32[8,16,2]{1,2,0:T(2,128)} %copy.603) | copy-start | bytes 3076
  454.5 21.1 %copy-start.18 = (f32[8,16,2]{1,2,0:T(2,128)S(1)}, f32[8,16,2]{1,2,0:T(2,128)}, u32[]{:S(2)}) copy-start(f32[8,16,2]{1,2,0:T(2,128)} %copy.605) | copy-start | bytes 3076
  454.6 21.1 %copy-start.19 = (f32[8,16,2]{1,2,0:T(2,128)S(1)}, f32[8,16,2]{1,2,0:T(2,128)}, u32[]{:S(2)}) copy-start(f32[8,16,2]{1,2,0:T(2,128)} %copy.607) | copy-start | bytes 3076
  454.6 21.1 %copy-start.20 = (f32[8,16,2]{1,2,0:T(2,128)S(1)}, f32[8,16,2]{1,2,0:T(2,128)}, u32[]{:S(2)}) copy-start(f32[8,16,2]{1,2,0:T(2,128)} %copy.609) | copy-start | bytes 3076
  454.6 21.1 %copy-start.21 = (f32[8,16,2]{1,2,0:T(2,128)S(1)}, f32[8,16,2]{1,2,0:T(2,128)}, u32[]{:S(2)}) copy-start(f32[8,16,2]{1,2,0:T(2,128)} %copy.611) | copy-start | bytes 3076
  454.6 21.1 %copy-start.22 = (f32[8,16,2]{1,2,0:T(2,128)S(1)}, f32[8,16,2]{1,2,0:T(2,128)}, u32[]{:S(2)}) copy-start(f32[8,16,2]{1,2,0:T(2,128)} %copy.613) | copy-start | bytes 3076
  454.6 21.1 %copy-start.23 = (f32[8,16,2]{1,2,0:T(2,128)S(1)}, f32[8,16,2]{1,2,0:T(2,128)}, u32[]{:S(2)}) copy-start(f32[8,16,2]{1,2,0:T(2,128)} %copy.615) | copy-start | bytes 3076
  454.6 21.1 %copy-start.24 = (f32[8,16,2]{1,2,0:T(2,128)S(1)}, f32[8,16,2]{1,2,0:T(2,128)}, u32[]{:S(2)}) copy-start(f32[8,16,2]{1,2,0:T(2,128)} %copy.617) | copy-start | bytes 3076
  454.6 21.1 %copy-start.25 = (f32[8,16,2]{1,2,0:T(2,128)S(1)}, f32[8,16,2]{1,2,0:T(2,128)}, u32[]{:S(2)}) copy-start(f32[8,16,2]{1,2,0:T(2,128)} %copy.619) | copy-start | bytes 3076
  454.6 21.1 %copy-start.26 = (f32[8,16,2]{1,2,0:T(2,128)S(1)}, f32[8,16,2]{1,2,0:T(2,128)}, u32[]{:S(2)}) copy-start(f32[8,16,2]{1,2,0:T(2,128)} %copy.621) | copy-start | bytes 3076
  454.6 21.1 %copy-start.27 = (f32[8,16,2]{1,2,0:T(2,128)S(1)}, f32[8,16,2]{1,2,0:T(2,128)}, u32[]{:S(2)}) copy-start(f32[8,16,2]{1,2,0:T(2,128)} %copy.623) | copy-start | bytes 3076
  466.4 20.9 %copy-start.46 = (f32[8,16,2]{1,2,0:T(2,128)S(1)}, f32[8,16,2]{1,2,0:T(2,128)}, u32[]{:S(2)}) copy-start(f32[8,16,2]{1,2,0:T(2,128)} %copy.675) | copy-start | bytes 3076
  466.4 20.9 %copy-start.47 = (f32[8,16,2]{1,2,0:T(2,128)S(1)}, f32[8,16,2]{1,2,0:T(2,128)}, u32[]{:S(2)}) copy-start(f32[8,16,2]{1,2,0:T(2,128)} %copy.677) | copy-start | bytes 3076
  466.5 20.9 %copy-start.48 = (f32[8,16,2]{1,2,0:T(2,128)S(1)}, f32[8,16,2]{1,2,0:T(2,128)}, u32[]{:S(2)}) copy-start(f32[8,16,2]{1,2,0:T(2,128)} %copy.679) | copy-start | bytes 3076
  466.5 20.9 %copy-start.49 = (f32[8,16,2]{1,2,0:T(2,128)S(1)}, f32[8,16,2]{1,2,0:T(2,128)}, u32[]{:S(2)}) copy-start(f32[8,16,2]{1,2,0:T(2,128)} %copy.681) | copy-start | bytes 3076
  466.5 20.9 %copy-start.50 = (f32[8,16,2]{1,2,0:T(2,128)S(1)}, f32[8,16,2]{1,2,0:T(2,128)}, u32[]{:S(2)}) copy-start(f32[8,16,2]{1,2,0:T(2,128)} %copy.683) | copy-start | bytes 3076
  466.5 20.9 %copy-start.51 = (f32[8,16,2]{1,2,0:T(2,128)S(1)}, f32[8,16,2]{1,2,0:T(2,128)}, u32[]{:S(2)}) copy-start(f32[8,16,2]{1,2,0:T(2,128)} %copy.685) | copy-start | bytes 3076
  466.5 20.9 %copy-start.52 = (f32[8,16,2]{1,2,0:T(2,128)S(1)}, f32[8,16,2]{1,2,0:T(2,128)}, u32[]{:S(2)}) copy-start(f32[8,16,2]{1,2,0:T(2,128)} %copy.687) | copy-start | bytes 3076
  466.5 20.9 %copy-start.53 = (f32[8,16,2]{1,2,0:T(2,128)S(1)}, f32[8,16,2]{1,2,0:T(2,128)}, u32[]{:S(2)}) copy-start(f32[8,16,2]{1,2,0:T(2,128)} %copy.689) | copy-start | bytes 3076
  620.3 175.5 %all-gather.6.cloned.1.call-start = ((), (), s32[]{:S(2)}) async-start(), calls=%async_computation.1 | async-start | bytes 9437184 | tf_op jit(solution)/shard_map/all_gather | solution.py:154
  636.9 284.6 %all-gather.8.cloned.1.call-start = ((), (), s32[]{:S(2)}) async-start(), calls=%async_computation.2 | async-start | bytes 9437184 | tf_op jit(solution)/shard_map/all_gather | solution.py:125
  639.3 428.9 %reduce-scatter.2.cloned.1.call-start = ((), (), s32[]{:S(2)}) async-start(), calls=%async_computation.3 | async-start | bytes 5242880 | tf_op jit(solution)/shard_map/reduce_scatter | solution.py:175
  (72 other events, 743.0 us)
Sparse Core Ops, SparseCore 0:
  620.5 49.7 all-gather.9
  672.4 123.3 all-gather.5
  797.9 123.5 all-gather.7
  1024.5 43.5 reduce-scatter.1

commit v2 on v1

--- a/solution.py
+++ b/solution.py
@@ -8,49 +8,61 @@
 highest = lax.Precision.HIGHEST
 
 
-def diagonal_blocks(matrix, size):
-    count = matrix.shape[0] // size
-    tiled = matrix.reshape(count, size, count, size)
-    mask = jnp.eye(count, dtype=bool)[:, None, :, None]
-    return jnp.sum(jnp.where(mask, tiled, 0.0), axis=2)
+def tile_inverse(tiles):
+    width = tiles.shape[-1]
+    row_ids = jnp.arange(width)[:, None]
+    col_ids = jnp.arange(width)[None, :]
+    identity = jnp.eye(width, dtype=jnp.float32)
+    leaf_part = jnp.where((row_ids // 8) == (col_ids // 8), tiles, 0.0)
+    square = jnp.matmul(leaf_part, leaf_part, precision=highest)
+    fourth = jnp.matmul(square, square, precision=highest)
+    inverse = jnp.matmul(identity - leaf_part, identity + square, precision=highest)
+    inverse = jnp.matmul(inverse, identity + fourth, precision=highest)
+    size = 8
+    while size < width:
+        pair_lower = (
+            ((row_ids // (2 * size)) == (col_ids // (2 * size)))
+            & ((row_ids // size) % 2 == 1)
+            & ((col_ids // size) % 2 == 0)
+        )
+        corner = jnp.where(pair_lower, tiles, 0.0)
+        inverse = inverse - jnp.matmul(
+            inverse, jnp.matmul(corner, inverse, precision=highest), precision=highest
+        )
+        size *= 2
+    return inverse
 
 
 def unit_lower_inverse(strict_lower):
     rows_total = strict_lower.shape[0]
-    leaf = 16
-    leaves = diagonal_blocks(strict_lower, leaf)
-    rows = []
-    for i in range(leaf):
-        row = jnp.broadcast_to((jnp.arange(leaf) == i).astype(jnp.float32), leaves.shape[:1] + (leaf,))
-        for m in range(i):
-            row = row - leaves[:, i, m][:, None] * rows[m]
-        rows.append(row)
-    inverse = jnp.stack(rows, axis=1)
-    size = leaf
+    tile = 128
+    count = rows_total // tile
+    blocks = [
+        strict_lower[q * tile:(q + 1) * tile, q * tile:(q + 1) * tile][None] for q in range(count)
+    ]
+    inverses = list(tile_inverse(jnp.concatenate(blocks, axis=0)))
+    size = tile
     while size < rows_total:
-        pairs = rows_total // (2 * size)
-        lower = diagonal_blocks(strict_lower, 2 * size)[:, size:, :size]
-        halves = inverse.reshape(pairs, 2, size, size)
-        first = halves[:, 0]
-        second = halves[:, 1]
-        corner = -jnp.einsum(
-            "pij,pjk->pik",
-            second,
-            jnp.einsum("pij,pjk->pik", lower, first, precision=highest),
-            precision=highest,
-        )
-        top = jnp.concatenate([first, jnp.zeros_like(first)], axis=2)
-        bottom = jnp.concatenate([corner, second], axis=2)
-        inverse = jnp.concatenate([top, bottom], axis=1)
+        merged = []
+        for p in range(len(inverses) // 2):
+            first = inverses[2 * p]
+            second = inverses[2 * p + 1]
+            start = 2 * p * size
+            lower = strict_lower[start + size:start + 2 * size, start:start + size]
+            corner = -jnp.dot(second, jnp.dot(lower, first, precision=highest), precision=highest)
+            top = jnp.concatenate([first, jnp.zeros_like(first)], axis=1)
+            bottom = jnp.concatenate([corner, second], axis=1)
+            merged.append(jnp.concatenate([top, bottom], axis=0))
+        inverses = merged
         size *= 2
-    return inverse[0]
+    return inverses[0]
 
 
 def lower_solve(strict_lower, right):
     rows_total = strict_lower.shape[0]
-    leaf = 16
-    count = rows_total // leaf
-    if rows_total % leaf or count & (count - 1):
+    tile = 128
+    count = rows_total // tile
+    if rows_total % tile or count & (count - 1):
         unit_lower = strict_lower + jnp.eye(rows_total, dtype=jnp.float32)
         return lax.linalg.triangular_solve(
             unit_lower, right, left_side=True, lower=True, unit_diagonal=True

time: 1100 us -> 605 us (0.55); the launches traced: 1080 us -> 594 us
  local copies, waits for them, and re-layouts: 449 us -> 35.6 us
  other arithmetic: 130 us -> 28.2 us
  matrix products: 215 us -> 250 us
    slice x132 -> x0, local copies, waits for them, and re-layouts: 217 us -> none  [the longest x127 211 us: unit_lower_inverse(): row = row - leaves[:, i, m][:, None] * rows[m]]
    mul x120 -> x0, local copies, waits for them, and re-layouts: 97 us -> none  [unit_lower_inverse(): row = row - leaves[:, i, m][:, None] * rows[m]]
    reshape x5 -> x0, local copies, waits for them, and re-layouts: 92.6 us -> none  [diagonal_blocks(): tiled = matrix.reshape(count, size, count, size)]
    reduce_sum x5 -> x0, other arithmetic: 64.2 us -> none  [diagonal_blocks(): return jnp.sum(jnp.where(mask, tiled, 0.0), axis=2)]
    dot_general x10 -> x18, matrix products: 23 us -> 60 us  [the longest x4 14.6 us: tile_inverse(): jnp.matmul(corner, inverse, precision=highest)]
    unnamed x14 -> x0, other arithmetic: 30.7 us -> none
  transfers between devices with their start and end apart: 4 -> 4, of which waited for: 3 -> 3; matrix products, arithmetic and copies ran while one was open for 7% -> 13% of each run, Pallas kernels for 0% -> 0%
where the time goes in v2:
time: 605 us; the launch traced here: 594 us
  matrix products  250 us (41%)
  waiting for transfers between devices  240 us (40%)
  local copies, waits for them, and re-layouts  35.6 us (6%)
  other arithmetic  28.2 us (5%)
  blocking collectives  24.8 us (4%)
  between operations  13.9 us (2%)
    all_gather x1, waiting for transfers between devices, on_device(): every_value = lax.all_gather(value_heads, 'ctx', axis=1, tiled=True)  126 us
    all_gather x1, waiting for transfers between devices, on_device(): every_key = lax.all_gather(keys_end, 'ctx', axis=1, tiled=True)  70.1 us
    reduce_scatter x1, waiting for transfers between devices, on_device(): lax.psum_scatter(jnp.dot(token_rows, out_weight, preferred_element_type=j...  43.8 us
    dot_general x7, matrix products, attend(): jnp.einsum('hqk,hkd->hqd', weights.astype(jnp.bfloat16), value_pair, pref...  30.4 us
    dot_general x1, matrix products, lower_solve(): return jnp.dot(unit_lower_inverse(strict_lower), right, precision=highest)  26.3 us
    all_gather x1, blocking collectives, on_device(): lax.all_gather(doc_float.astype(jnp.bfloat16), 'ctx', axis=0, tiled=True)  24.8 us
    dot_general x7, matrix products, attend(): turned = jnp.einsum('hqd,hde->hqe', turned, transfer_in, precision=highest)  23.9 us
    unnamed x48, local copies, waits for them, and re-layouts  20.1 us
  transfers between devices with their start and end apart: 4, of which 3 were waited for; matrix products, arithmetic and copies ran while one was open for 13% of the time, Pallas kernels for 0%

profile of v2, /device:TPU:16, one launch (start us, length us, event | category | flops | bytes accessed | tf_op | source)
XLA Modules:
  0.0 593.5 jit_solution(11215840952575589839)
XLA Ops:
  11.5 7.5 %multiply_select_fusion.1 = f32[8,512,512]{1,2,0:T(8,128)S(1)} fusion(f32[8,512]{1,0:T(8,128)S(1)} %multiply_bitcast_fusion, pred[512,512]{0,1:T(8,128)(4,1)S(1)} %iota_compare_fusion.3, f32[8,512,128]{1,2,0:T(8,128)S(1)} %broadcast_divide_fusion), kind=kOutput, calls=%fused_computation.44 | convolution fusion | flops 3225419776 | bytes 10764288 | tf_op jit(solution)/shard_map/vmap()/dot_general | solution.py:79
  24.0 5.2 fusion.75
  32.2 4.4 convolution_add_fusion
  40.3 4.5 fusion.71
  76.6 6.3 %fusion.55 = f32[8,256,256]{1,2,0:T(8,128)} fusion(f32[8,512,512]{1,2,0:T(8,128)} %copy-done.2, f32[8,128,128]{2,1,0:T(8,128)S(1)} %get-tuple-element.259, f32[8,128,128]{2,1,0:T(8,128)S(1)} %get-tuple-element.258, f32[8,128,128]{2,1,0:T(8,128)S(1)} %convolution_negate_fusion.1), kind=kOutput, calls=%fused_computation.64 | convolution fusion | flops 1612709888 | bytes 5767168 | tf_op jit(solution)/shard_map/vmap()/dot_general | solution.py:52
  91.5 6.1 %broadcast_select_fusion = f32[8,512,512]{1,2,0:T(8,128)} fusion(pred[512,512]{0,1:T(8,128)(4,1)S(1)} %iota_compare_fusion.3, f32[8,512,128]{1,2,0:T(8,128)S(1)} %broadcast_divide_fusion, bf16[512,8,128]{2,0,1:T(8,128)(2,1)S(1)} %copy.112), kind=kOutput, calls=%fused_computation.60 | convolution fusion | flops 3223322624 | bytes 11796480 | tf_op jit(solution)/shard_map/vmap()/dot_general | solution.py:81
  102.2 26.3 %fusion.22 = f32[8,512,640]{2,1,0:T(8,128)} fusion(f32[8,512,128]{1,2,0:T(8,128)S(1)} %broadcast_divide_fusion, f32[8,512,512]{1,2,0:T(8,128)} %broadcast_select_fusion, f32[8,256,256]{2,1,0:T(8,128)} %select_maximum_fusion.2, f32[8,128,128]{2,1,0:T(8,128)} %get-tuple-element.260, f32[8,128,128]{2,1,0:T(8,128)} %convolution_negate_fusion, ...), kind=kOutput, calls=%fused_computation.26 | convolution fusion | flops 16121331712 | bytes 27262976 | tf_op jit(solution)/shard_map/vmap()/dot_general | solution.py:70
  134.6 4.4 fusion.93
  139.1 16.4 %subtract_convert_fusion = bf16[8,512,128]{2,1,0:T(8,128)(2,1)} fusion(f32[8,512,128]{1,2,0:T(8,128)S(1)} %broadcast_divide_fusion, f32[8,512,640]{2,1,0:T(8,128)} %fusion.22, bf16[512,8,128]{2,0,1:T(8,128)(2,1)S(1)} %copy.112, f32[8,512]{1,0:T(8,128)S(1)} %multiply_bitcast_fusion), kind=kOutput, calls=%fused_computation.91 | convolution fusion | flops 3223322624 | bytes 12599296 | tf_op jit(solution)/shard_map/vmap()/dot_general | solution.py:86
  163.0 4.9 fusion.99
  171.2 16.7 %convert_subtract_fusion = f32[8,512,128]{2,1,0:T(8,128)} fusion(f32[8,512,512]{2,1,0:T(8,128)S(1)} %fusion.99, f32[8,512]{1,0:T(8,128)S(1)} %multiply_bitcast_fusion, pred[512,512]{0,1:T(8,128)(4,1)S(1)} %iota_compare_fusion.4, bf16[512,8,128]{2,0,1:T(8,128)(2,1)S(1)} %copy-done.5, f32[8,512,640]{2,1,0:T(8,128)} %fusion.22), kind=kOutput, calls=%fused_computation.96 | convolution fusion | flops 3226468352 | bytes 13910016 | tf_op jit(solution)/shard_map/vmap()/dot_general | solution.py:95
  189.9 24.8 %all-gather.1 = bf16[8,1,512]{2,1,0:T(2,128)(2,1)S(1)} all-gather(bf16[1,1,512]{2,1,0:T(2,128)(2,1)S(1)} %reshape.609), channel_id=1, replica_groups=mesh['ctx'=8,'head'=4] {'ctx'}, dimensions={0}, use_global_device_ids=true | all-gather | bytes 9216 | tf_op jit(solution)/shard_map/all_gather | solution.py:171
  214.9 19.1 %fusion.37 = f32[8,512,512]{1,2,0:T(8,128)S(1)} fusion(f32[8,512,640]{2,1,0:T(8,128)} %fusion.22, f32[8,512,512]{2,1,0:T(8,128)} %copy-done, f32[8,512]{1,0:T(8,128)S(1)} %multiply_bitcast_fusion, pred[512,512]{0,1:T(8,128)(4,1)S(1)} %iota_compare_fusion.4), kind=kOutput, calls=%fused_computation.47 | convolution fusion | flops 12889096192 | bytes 25444352 | tf_op jit(solution)/shard_map/vmap()/dot_general | solution.py:92
  244.4 70.1 %all-gather.6.cloned.1.call-done = bf16[8,4096,128]{2,1,0:T(8,128)(2,1)} async-done(((bf16[8,512,128]{2,1,0:T(8,128)(2,1)}), bf16[8,4096,128]{2,1,0:T(8,128)(2,1)}) %all-gather.6.cloned.1.call-update) | async-done | bytes 8388624 | tf_op jit(solution)/shard_map/all_gather | solution.py:166
  314.5 125.7 %all-gather.8.cloned.1.call-done = bf16[8,4096,128]{1,2,0:T(8,128)(2,1)} async-done(((bf16[8,512,128]{1,2,0:T(8,128)(2,1)}), bf16[8,4096,128]{1,2,0:T(8,128)(2,1)}) %all-gather.8.cloned.1.call-update) | async-done | bytes 8388624 | tf_op jit(solution)/shard_map/all_gather | solution.py:137
  440.2 91.1 %while.19 = (s32[]{:T(128)}, f32[8,512,128]{1,2,0:T(8,128)S(1)}, f32[8,512]{1,0:T(8,128)S(1)}, f32[8,512]{1,0:T(8,128)S(1)}, f32[8,512,128]{2,1,0:T(8,128)}, /*i...) while((s32[]{:T(128)}, f32[8,512,128]{1,2,0:T(8,128)S(1)}, ...), condition=%wide.region_6.7_spmd, body=%wide.region_3.6_spmd.sunk | while | flops 1904222208 | bytes 60563748 | solution.py:184
  445.5 4.3 multiply_add_fusion.5
  458.5 4.3 multiply_add_fusion.5
  471.5 4.3 multiply_add_fusion.5
  484.5 4.3 multiply_add_fusion.5
  497.5 4.3 multiply_add_fusion.5
  510.5 4.3 multiply_add_fusion.5
  533.5 9.5 %convolution_convert_fusion = bf16[512,4096]{1,0:T(8,128)(2,1)} fusion(bf16[512,1024]{0,1:T(8,128)(2,1)S(1)} %bitcast.129, bf16[1024,4096]{1,0:T(8,128)(2,1)} %param.15), kind=kOutput, calls=%fused_computation.52 | convolution fusion | flops 4297064448 | bytes 13631488 | tf_op jit(solution)/shard_map/dot_general | solution.py:188
  543.0 43.8 %reduce-scatter.2.cloned.1.call-done = bf16[128,4096]{1,0:T(8,128)(2,1)} async-done(((bf16[512,4096]{1,0:T(8,128)(2,1)}), bf16[128,4096]{1,0:T(8,128)(2,1)}) %reduce-scatter.2.cloned.1.call-update) | async-done | bytes 1048592 | tf_op jit(solution)/shard_map/reduce_scatter | solution.py:187
  (204 shorter events, 156.8 us)
Async XLA Ops:
  6.5 233.8 %all-gather.10.cloned.1.call-start = ((), (), s32[]{:S(2)}) async-start(), calls=%async_computation.4 | async-start | bytes 2359296 | tf_op jit(solution)/shard_map/all_gather | solution.py:168
  19.0 4.5 copy-start.2
  19.3 4.5 copy-start.13
  19.3 4.7 copy-start.15
  32.2 4.4 copy-start.1
  32.2 4.4 copy-start.10
  40.2 4.8 copy-start.14
  40.3 4.8 copy-start.16
  69.7 5.8 copy-start.3
  91.5 6.1 %copy-start.20 = (f32[8,128,128]{2,1,0:T(8,128)S(1)}, f32[8,128,128]{2,1,0:T(8,128)}, u32[]{:S(2)}) copy-start(f32[8,128,128]{2,1,0:T(8,128)} %get-tuple-element.257) | copy-start | bytes 1572868
  91.5 7.2 %copy-start.9 = (f32[8,256,256]{1,2,0:T(8,128)S(1)}, f32[8,256,256]{1,2,0:T(8,128)}, u32[]{:S(2)}) copy-start(f32[8,256,256]{1,2,0:T(8,128)} %fusion.55) | copy-start | bytes 6291460
  91.5 7.2 %copy-start.18 = (f32[8,128,128]{2,1,0:T(8,128)S(1)}, f32[8,128,128]{2,1,0:T(8,128)}, u32[]{:S(2)}) copy-start(f32[8,128,128]{2,1,0:T(8,128)} %convolution_negate_fusion) | copy-start | bytes 1572868
  91.5 7.2 %copy-start.19 = (f32[8,128,128]{2,1,0:T(8,128)S(1)}, f32[8,128,128]{2,1,0:T(8,128)}, u32[]{:S(2)}) copy-start(f32[8,128,128]{2,1,0:T(8,128)} %get-tuple-element.260) | copy-start | bytes 1572868
  139.0 175.5 %all-gather.6.cloned.1.call-start = ((), (), s32[]{:S(2)}) async-start(), calls=%async_computation.1 | async-start | bytes 9437184 | tf_op jit(solution)/shard_map/all_gather | solution.py:166
  155.6 284.6 %all-gather.8.cloned.1.call-start = ((), (), s32[]{:S(2)}) async-start(), calls=%async_computation.2 | async-start | bytes 9437184 | tf_op jit(solution)/shard_map/all_gather | solution.py:137
  157.9 428.8 %reduce-scatter.2.cloned.1.call-start = ((), (), s32[]{:S(2)}) async-start(), calls=%async_computation.3 | async-start | bytes 5242880 | tf_op jit(solution)/shard_map/reduce_scatter | solution.py:187
  163.0 8.2 %copy-start.5 = (bf16[512,8,128]{2,0,1:T(8,128)(2,1)S(1)}, bf16[512,8,128]{2,0,1:T(8,128)(2,1)}, u32[]{:S(2)}) copy-start(bf16[512,8,128]{2,0,1:T(8,128)(2,1)} %copy.80) | copy-start | bytes 3145732
  214.9 19.2 %copy-start.6 = (bf16[512,8,128]{2,0,1:T(8,128)(2,1)S(1)}, bf16[512,8,128]{2,0,1:T(8,128)(2,1)}, u32[]{:S(2)}) copy-start(bf16[512,8,128]{2,0,1:T(8,128)(2,1)} %copy.80) | copy-start | bytes 3145732
  449.9 3.4 copy-start.12
  462.9 3.4 copy-start.12
  475.9 3.4 copy-start.12
  488.9 3.4 copy-start.12
  501.8 3.4 copy-start.12
  527.8 3.4 copy-start.12
  (15 other events, 28.9 us)
Sparse Core Ops, SparseCore 0:
  139.2 49.7 all-gather.9
  191.2 123.3 all-gather.5
  316.6 123.5 all-gather.7
  543.1 43.5 reduce-scatter.1
